TPU v7x, 128 devices: a whole 4x4x4 slice. The times are simulated.
128 devices in a mesh: req: 32 (over x, y, core), tp: 4 (over z).
Axes of the slice: x: 4, y: 4, z: 4, core: 2. Of those that a mesh axis runs over, the one named last changes fastest.
Arguments:
- stream: bfloat16 [64, 64, 3584], P('req'), may hold values from -40 to 40
- queries: bfloat16 [64, 64, 3584], P('req', None, 'tp'), may hold values from -4 to 4
- key_new: bfloat16 [64, 64, 3584], P('req', None, 'tp'), may hold values from -18 to 18
- value_new: bfloat16 [64, 64, 3584], P('req', None, 'tp'), may hold values from -6 to 6
- cache_key: bfloat16 [64, 1024, 3584], P('req', None, 'tp'), may hold values from -5 to 5
- cache_value: bfloat16 [64, 1024, 3584], P('req', None, 'tp'), may hold values from -6 to 6
- cache_length: int32 [64], P('req'), may hold values from 64 to 1024, as said below
- parents: int32 [64, 64], P('req'), may hold values from -1 to 62, as said below
- accept: int32 [64, 8, 64], P('req'), may hold values from 0 to 1, as said below
- out_weight: bfloat16 [3584, 3584], P('tp'), may hold values from -0.75 to 0.75
- norm_gain: float32 [3584], replicated, may hold values from 0.1 to 1.9
- head_weight: bfloat16 [32000, 3584], P('req'), may hold values from -1 to 1
- candidate: int32 [64, 64], replicated, may hold values from 0 to 31999
- dealing: int32 [64], replicated, may hold values from 0 to 63, each once
Outputs:
- target_logprob: float32 [64, 64], P('req')
- accepted_state: bfloat16 [64, 8, 3584], P('req', None, 'tp')
Inputs may be any that keep to these rules, and one draw needn't show every extreme that they name: `cache_length`: every cache holds at least 64 live positions; in every draw some slot's cache is full. `parents`: node 0 is the root with parent -1; node t > 0 lies at depth (t - 1) // 9 + 1 and its parent lies one depth above it. `accept`: row a of a slot's matrix is one-hot on the node at depth a of the accepted path, which runs from the root down the slot's tree to some node; rows past the path's end are zero; in every draw some path ends at the deepest level.
All inputs are finite; a program needn't handle non-finite values.
Results may differ from a plain program's by a relative error of at most 0.012.
Values may be sent and summed in bfloat16 or wider, within the bound.
No kernel may reach another device: no remote copies, remote signals or barrier semaphores. Data moves between devices by JAX's collectives and lax.ppermute only.
A program may use at most 192 MiB of HBM per device.

v0:
```python
import jax
import jax.numpy as jnp
from jax import lax
from jax.sharding import PartitionSpec as P

HD = 224
ACC = 8
EPS = 1e-05
HIGH = lax.Precision.HIGHEST
block_limit = 512


def combined_all(value, axis, join):
    pieces = jax.tree.map(lambda part: lax.all_gather(part, axis), value)
    head = jax.tree.map(lambda part: part[0], pieces)
    tail = jax.tree.map(lambda part: part[1:], pieces)
    subtotal, _ = lax.scan(lambda subtotal, share: (join(subtotal, share), None), head, tail)
    return subtotal


def ancestry(parents):
    node_count = parents.shape[-1]
    node_ids = jnp.arange(node_count, dtype=jnp.int32)
    stride_map = (parents[..., :, None] == node_ids).astype(jnp.float32)
    reached = jnp.broadcast_to(jnp.eye(node_count, dtype=jnp.float32), stride_map.shape) > 0.5
    for doubling in range((ACC - 1).bit_length()):
        further = lax.optimization_barrier(
            jnp.einsum("rtk,rku->rtu", reached.astype(jnp.float32), stride_map, precision=HIGH)
        )
        reached = jnp.logical_or(reached, further > 0.5)
        stride_map = jnp.einsum("rtk,rku->rtu", stride_map, stride_map, precision=HIGH)
    return reached


def combine_stats(earlier, later):
    joint_max = jnp.maximum(earlier[0], later[0])
    joint_sum = earlier[1] * jnp.exp(earlier[0] - joint_max) + later[1] * jnp.exp(
        later[0] - joint_max
    )
    return (joint_max, joint_sum, earlier[2] + later[2])


def vocab_stats(logits, vocab_ids, wanted, along):
    row_max = jnp.max(logits, axis=along)
    row_sum = jnp.sum(jnp.exp(logits - jnp.expand_dims(row_max, along)), axis=along)
    matches = jnp.expand_dims(vocab_ids, 1 - along) == jnp.expand_dims(wanted, along)
    picked = jnp.sum(jnp.where(matches, logits, 0.0), axis=along)
    return (row_max, row_sum, picked)


def local(
    stream,
    queries,
    key_new,
    value_new,
    cache_key,
    cache_value,
    cache_length,
    parents,
    accept,
    out_weight,
    norm_gain,
    head_weight,
    candidate,
    dealing,
):
    slots, tree_size, qwidth = queries.shape
    model_width = stream.shape[2]
    heads_loc = qwidth // HD
    n_tp = lax.axis_size("tp")
    n_req = lax.axis_size("req")
    tp_id = lax.axis_index("tp")
    req_id = lax.axis_index("req")
    score_scale = HD ** (-0.5)
    query_rows = queries.reshape(slots, tree_size, heads_loc, HD)
    tree_keys = key_new.reshape(slots, tree_size, heads_loc, HD)
    tree_values = value_new.reshape(slots, tree_size, heads_loc, HD)
    visible = ancestry(parents)
    tree_scores = (
        jnp.einsum("rthd,rkhd->rhtk", query_rows, tree_keys, preferred_element_type=jnp.float32)
        * score_scale
    )
    tree_scores = jnp.where(visible[:, None], tree_scores, -jnp.inf)
    running_max = jnp.max(tree_scores, axis=3)
    weights = jnp.exp(tree_scores - running_max[..., None])
    running_sum = jnp.sum(weights, axis=3)
    running_out = jnp.einsum(
        "rhtk,rkhd->rhtd",
        weights.astype(jnp.bfloat16),
        tree_values,
        preferred_element_type=jnp.float32,
    )
    cache_cap = cache_key.shape[1]
    block_rows = min(block_limit, cache_cap)
    block_count = (jnp.max(cache_length) + block_rows - 1) // block_rows

    def visit_block(block_index, folded):
        old_max, old_sum, old_out = folded
        offset = block_index * block_rows
        past_keys = lax.dynamic_slice_in_dim(cache_key, offset, block_rows, 1).reshape(
            slots, block_rows, heads_loc, HD
        )
        past_values = lax.dynamic_slice_in_dim(cache_value, offset, block_rows, 1).reshape(
            slots, block_rows, heads_loc, HD
        )
        scores = (
            jnp.einsum("rthd,rkhd->rhtk", query_rows, past_keys, preferred_element_type=jnp.float32)
            * score_scale
        )
        live_mask = (offset + jnp.arange(block_rows, dtype=jnp.int32))[None, :] < cache_length[
            :, None
        ]
        scores = jnp.where(live_mask[:, None, None, :], scores, -jnp.inf)
        new_max = jnp.maximum(old_max, jnp.max(scores, axis=3))
        shrink = jnp.exp(old_max - new_max)
        block_weights = jnp.exp(scores - new_max[..., None])
        new_sum = old_sum * shrink + jnp.sum(block_weights, axis=3)
        contribution = lax.optimization_barrier(
            jnp.einsum(
                "rhtk,rkhd->rhtd",
                block_weights.astype(jnp.bfloat16),
                past_values,
                preferred_element_type=jnp.float32,
            )
        )
        new_out = old_out * shrink[..., None] + contribution
        return (new_max, new_sum, new_out)

    running_max, running_sum, running_out = lax.fori_loop(
        0, block_count, visit_block, (running_max, running_sum, running_out)
    )
    attention = (running_out / running_sum[..., None]).astype(jnp.bfloat16)
    attention_rows = attention.transpose(0, 2, 1, 3).reshape(slots * tree_size, qwidth)
    flat_stream = stream.reshape(slots * tree_size, model_width)
    rows_all = slots * tree_size
    quarter = rows_all // n_tp
    dslice = model_width // n_tp
    partial_out = jnp.dot(attention_rows, out_weight, preferred_element_type=jnp.float32)
    summed = lax.psum_scatter(
        partial_out.astype(jnp.bfloat16), "tp", scatter_dimension=1, tiled=True
    ).astype(jnp.float32)
    own_stream = lax.dynamic_slice_in_dim(flat_stream, tp_id * dslice, dslice, 1)
    post_rows = (own_stream.astype(jnp.float32) + summed).astype(jnp.bfloat16)
    post_float = post_rows.astype(jnp.float32)
    square = jnp.sum(post_float * post_float, axis=1)
    energy = lax.psum(square, "tp")
    inverse = lax.rsqrt(energy / model_width + EPS)
    part_gain = lax.dynamic_slice_in_dim(norm_gain, tp_id * dslice, dslice, 0)
    normed_slice = (post_float * inverse[:, None] * part_gain[None, :]).astype(jnp.bfloat16)
    compact = jnp.einsum(
        "sat,std->sad",
        accept.astype(jnp.bfloat16),
        post_rows.reshape(slots, tree_size, dslice),
        preferred_element_type=jnp.float32,
    ).astype(jnp.bfloat16)
    normed = lax.all_to_all(normed_slice, "tp", split_axis=0, concat_axis=1, tiled=True)
    vocab_loc = head_weight.shape[0]
    wanted_rows = lax.dynamic_slice_in_dim(
        candidate.reshape(n_req, rows_all), tp_id * quarter, quarter, 1
    ).reshape(-1)
    vocab_ids = req_id * vocab_loc + jnp.arange(vocab_loc, dtype=jnp.int32)
    logits = lax.dot_general(
        lax.all_gather(normed, "req", axis=0, tiled=True),
        head_weight,
        (((1,), (1,)), ((), ())),
        preferred_element_type=jnp.float32,
    )
    found_stats = vocab_stats(logits, vocab_ids, wanted_rows, 1)
    local_stats = tuple((after_part for after_part in found_stats))
    merged = combined_all((local_stats[0], local_stats[1], local_stats[2]), "req", combine_stats)
    all_stats = (
        lax.all_gather(merged[0], "tp", axis=0, tiled=True),
        lax.all_gather(merged[1], "tp", axis=0, tiled=True),
        lax.all_gather(merged[2], "tp", axis=0, tiled=True),
    )
    row_max, row_sum, picked = tuple(
        (
            member.reshape(n_tp, n_req, quarter).transpose(1, 0, 2).reshape(-1)
            for member in all_stats
        )
    )
    logprob = (picked - row_max - jnp.log(row_sum)).reshape(-1, tree_size)
    own_requests = req_id * slots + jnp.arange(slots, dtype=jnp.int32)
    selector = dealing[None, :] == own_requests[:, None]
    target_logprob = jnp.dot(selector.astype(jnp.float32), logprob, precision=HIGH)
    home_states = lax.all_gather(compact, "req", axis=0, tiled=True)
    accepted_state = jnp.einsum(
        "ks,sad->kad",
        selector.astype(jnp.bfloat16),
        home_states,
        preferred_element_type=jnp.float32,
    ).astype(jnp.bfloat16)
    return (target_logprob, accepted_state)


def solution(mesh):
    placed = (
        P("req", None, None),
        P("req", None, "tp"),
        P("req", None, "tp"),
        P("req", None, "tp"),
        P("req", None, "tp"),
        P("req", None, "tp"),
        P("req"),
        P("req", None),
        P("req", None, None),
        P("tp", None),
        P(),
        P("req", None),
        P(),
        P(),
    )
    return jax.shard_map(
        local,
        mesh=mesh,
        in_specs=placed,
        out_specs=(P("req", None), P("req", None, "tp")),
        check_vma=False,
    )
```

profile of v0, /device:TPU:0, one launch (start us, length us, event | category | flops | bytes accessed | tf_op | source)
XLA Modules:
  0.0 275.6 jit_solution(6451548967636028759)
XLA Ops:
  7.2 0.0 reduce-scatter.4.cloned.1.call-start
  7.2 1.4 reduce_max.37
  9.3 1.0 fusion.21
  10.3 0.2 fusion.38
  10.5 0.9 fusion.22
  11.4 0.2 fusion.37
  11.6 0.2 fusion.39
  11.8 0.1 copy.47
  11.9 1.2 reshape.97
  13.1 0.7 copy.48
  13.9 1.2 reshape.98
  15.1 1.2 reshape.99
  16.3 0.2 fusion.35
  16.5 0.1 fusion.18
  16.6 0.3 fusion.13
  16.9 12.5 %while.28 = (s32[]{:T(128)}, f32[2,4,64]{2,1,0:T(4,128)S(1)}, f32[2,4,64]{2,1,0:T(4,128)S(1)}, f32[2,4,64,224]{3,2,1,0:T(8,128)S(1)}, s32[]{:T(128)}, /*index=5*...) while((s32[]{:T(128)}, f32[2,4,64]{2,1,0:T(4,128)S(1)}, ...), condition=%wide.region_6.7_spmd, body=%wide.region_3.6_spmd.sunk | while | flops 236947968 | bytes 23599292 | solution.py:129
  16.9 0.1 broadcast_compare_fusion.2
  17.0 4.1 %constant_dynamic-slice_fusion.9 = (bf16[2,512,896]{2,1,0:T(8,128)(2,1)}, bf16[2,512,896]{2,1,0:T(8,128)(2,1)}) fusion(bf16[2,1024,896]{2,1,0:T(8,128)(2,1)} %get-tuple-element.346, s32[]{:T(128)S(6)} %select_n.42, bf16[2,1024,896]{2,1,0:T(8,128)(2,1)} %get-tuple-element.344), kind=kLoop, calls=%fused_computation.13.clone.1 | loop fusion | bytes 7340036 | tf_op jit(solution)/shard_map/while/body/dynamic_slice | solution.py:103
  21.1 2.7 copy.80
  23.9 1.5 fusion.66
  25.4 0.3 fusion.67
  25.8 2.8 copy.81
  28.5 0.7 fusion.68
  29.2 0.2 multiply_add_fusion.7
  29.4 0.1 fusion.16
  29.6 0.2 copy.55
  29.8 0.2 reshape.100
  30.0 4.0 %convolution_convert_fusion = bf16[128,3584]{1,0:T(8,128)(2,1)S(1)} fusion(bf16[128,896]{1,0:T(8,128)(2,1)S(1)} %reshape.100, bf16[896,3584]{1,0:T(8,128)(2,1)} %param.27), kind=kOutput, calls=%fused_computation.19 | convolution fusion | flops 822542336 | bytes 7569408 | tf_op jit(solution)/shard_map/dot_general | solution.py:138
  34.0 0.0 copy-start
  34.0 0.0 copy-start.2
  34.0 0.0 copy-start.3
  34.0 1.3 copy.61
  35.3 0.0 reduce-scatter.4.cloned.1.call-update
  35.3 0.0 all-gather.5.cloned.1.call-start
  35.4 0.8 dynamic_slice.26
  36.1 37.4 %reduce-scatter.4.cloned.1.call-done = bf16[896,128]{1,0:T(8,128)(2,1)} async-done(((bf16[3584,128]{1,0:T(8,128)(2,1)}), bf16[896,128]{1,0:T(8,128)(2,1)}) %reduce-scatter.4.cloned.1.call-update) | async-done | bytes 229392
  73.5 1.1 copy.62
  74.6 1.1 fusion.10
  75.7 8.0 %psum.7 = f32[128]{0:T(128)S(1)} all-reduce(f32[128]{0:T(128)S(1)} %get-tuple-element.177), channel_id=1, replica_groups=mesh['req'=32,'tp'=4] {'tp'}, use_global_device_ids=true, to_apply=%region_9.10 | all-reduce | flops 128 | bytes 1024 | tf_op jit(solution)/shard_map/psum | solution.py:146
  83.7 0.1 fusion.12
  83.9 9.3 %all_to_all.19 = bf16[4,32,896]{2,1,0:T(8,128)(2,1)S(1)} all-to-all(bf16[4,32,896]{2,1,0:T(8,128)(2,1)S(1)} %bitcast.79), channel_id=1, replica_groups=mesh['req'=32,'tp'=4] {'tp'}, dimensions={0} | all-to-all | bytes 458752 | tf_op jit(solution)/shard_map/all_to_all | solution.py:156
  93.2 0.7 copy.65
  93.9 0.0 all-gather.5.cloned.1.call-update
  93.9 0.1 reshape.101
  94.0 0.1 constant_dynamic-slice_fusion.5
  94.1 0.1 eq.54
  94.2 0.1 fusion.8
  94.3 25.4 %all_gather.43 = bf16[64,8,896]{2,1,0:T(8,128)(2,1)S(1)} all-gather(bf16[2,8,896]{2,1,0:T(8,128)(2,1)S(1)} %fusion.8), channel_id=1, replica_groups=mesh['req'=32,'tp'=4] {'req'}, dimensions={0}, use_global_device_ids=true | all-gather | bytes 946176 | tf_op jit(solution)/shard_map/all_gather | solution.py:186
  119.7 0.3 convolution_convert_fusion.1
  120.0 0.6 copy.59
  120.7 23.6 %all-gather.5.cloned.1.call-done = bf16[1024,3584]{1,0:T(8,128)(2,1)} async-done(((bf16[32,3584]{1,0:T(8,128)(2,1)}), bf16[1024,3584]{1,0:T(8,128)(2,1)}) %all-gather.5.cloned.1.call-update) | async-done | bytes 7340048 | tf_op jit(solution)/shard_map/all_gather | solution.py:163
  144.2 12.1 %fusion.36 = (f32[1024]{0:T(1024)S(1)}, f32[1024,1000]{0,1:T(8,128)S(1)}) fusion(bf16[1024,3584]{1,0:T(8,128)(2,1)} %all-gather.5.cloned.1.call-done, bf16[1000,3584]{1,0:T(8,128)(2,1)} %param.29), kind=kOutput, calls=%fused_computation.70 | convolution fusion | flops 7341054976 | bytes 18608128 | tf_op jit(solution)/shard_map/dot_general | solution.py:162
  156.3 1.4 select_reduce_fusion
  157.7 24.1 %all-gather.2 = f32[32768]{0:T(1024)S(1)} all-gather(f32[1024]{0:T(1024)S(1)} %get-tuple-element.139), channel_id=4, replica_groups=mesh['req'=32,'tp'=4] {'req'}, dimensions={0}, use_global_device_ids=true | all-gather | bytes 135168 | tf_op jit(solution)/shard_map/all_gather | solution.py:14
  181.8 22.7 %all-gather = f32[32768]{0:T(1024)S(1)} all-gather(f32[1024]{0:T(1024)S(1)} %get-tuple-element.187), channel_id=2, replica_groups=mesh['req'=32,'tp'=4] {'req'}, dimensions={0}, use_global_device_ids=true | all-gather | bytes 135168 | tf_op jit(solution)/shard_map/all_gather | solution.py:14
  204.5 23.8 %all-gather.1 = f32[32768]{0:T(1024)S(1)} all-gather(f32[1024]{0:T(1024)S(1)} %get-tuple-element.140), channel_id=3, replica_groups=mesh['req'=32,'tp'=4] {'req'}, dimensions={0}, use_global_device_ids=true | all-gather | bytes 135168 | tf_op jit(solution)/shard_map/all_gather | solution.py:14
  228.4 2.8 %while.29 = (s32[]{:T(128)}, f32[1024]{0:T(1024)S(1)}, f32[1024]{0:T(1024)S(1)}, f32[1024]{0:T(1024)S(1)}, f32[31,1024]{1,0:T(8,128)S(1)}, /*index=5*/f32[31,1024]{1,0:T(8,128)S(1)}, f32[31,1024]{1,0:T(8,128)S(1)}, s32[]{:T(128)}) while((s32[]{:T(128)}, f32[1024]{0:T(1024)S(1)}, f32[1024]{0:T(1024)S(1)}, f32[1024]{0:T(1024)S(1)}, ...), condition=%wide.region_14.15_spmd, body=%wide.region_13.14_spmd.sunk | while | flops 7170 | bytes 61541 | solution.py:17
  231.2 12.5 %all_gather.40 = f32[4096]{0:T(1024)S(1)} all-gather(f32[1024]{0:T(1024)S(1)} %get-tuple-element.92), channel_id=1, replica_groups=mesh['req'=32,'tp'=4] {'tp'}, dimensions={0}, use_global_device_ids=true | all-gather | bytes 20480 | tf_op jit(solution)/shard_map/all_gather | solution.py:174
  243.7 12.0 %all_gather.41 = f32[4096]{0:T(1024)S(1)} all-gather(f32[1024]{0:T(1024)S(1)} %get-tuple-element.93), channel_id=1, replica_groups=mesh['req'=32,'tp'=4] {'tp'}, dimensions={0}, use_global_device_ids=true | all-gather | bytes 20480 | tf_op jit(solution)/shard_map/all_gather | solution.py:172
  255.7 12.0 %all_gather.42 = f32[4096]{0:T(1024)S(1)} all-gather(f32[1024]{0:T(1024)S(1)} %get-tuple-element.94), channel_id=1, replica_groups=mesh['req'=32,'tp'=4] {'tp'}, dimensions={0}, use_global_device_ids=true | all-gather | bytes 20480 | tf_op jit(solution)/shard_map/all_gather | solution.py:173
  267.8 0.1 sub.68
  267.8 0.1 copy.57
  267.9 0.1 sub.70
  268.0 0.8 fusion.27
  (149 shorter events, 1.7 us)
Async XLA Ops:
  7.2 9.7 %copy-start.1 = (s32[2]{0:T(128)S(1)}, s32[2]{0:T(128)}, u32[]{:S(2)}) copy-start(s32[2]{0:T(128)} %param.24) | copy-start | bytes 28
  7.2 66.4 %reduce-scatter.4.cloned.1.call-start = ((), (), s32[]{:S(2)}) async-start(), calls=%async_computation.3 | async-start | bytes 1146880
  34.0 60.0 %copy-start = (s32[64,64]{1,0:T(8,128)S(1)}, s32[64,64]{1,0:T(8,128)}, u32[]{:S(2)}) copy-start(s32[64,64]{1,0:T(8,128)} %param.30) | copy-start | bytes 49156
  34.0 60.2 %copy-start.2 = (s32[2,8,64]{2,1,0:T(8,128)S(1)}, s32[2,8,64]{2,1,0:T(8,128)}, u32[]{:S(2)}) copy-start(s32[2,8,64]{2,1,0:T(8,128)} %param.26) | copy-start | bytes 12292
  34.0 85.8 %copy-start.3 = (s32[64]{0:T(128)S(1)}, s32[64]{0:T(128)}, u32[]{:S(2)}) copy-start(s32[64]{0:T(128)} %param.31) | copy-start | bytes 772
  35.3 108.9 %all-gather.5.cloned.1.call-start = ((), (), s32[]{:S(2)}) async-start(), calls=%async_computation.2 | async-start | bytes 7569408 | tf_op jit(solution)/shard_map/all_gather | solution.py:163
Sparse Core Ops, SparseCore 0:
  35.4 38.0 reduce-scatter.3
  94.1 50.1 all-gather.4
where the time goes:
time: 276 us
  blocking collectives  150 us (54%)
  waiting for transfers between devices  61 us (22%)
  matrix products  22.3 us (8%)
  local copies, waits for them, and re-layouts  20.5 us (7%)
  between operations  15 us (5%)
  other arithmetic  5.41 us (2%)
    all_gather x3, blocking collectives, combined_all(): pieces = jax.tree.map(lambda part: lax.all_gather(part, axis), value)  70.6 us
    unnamed x3, waiting for transfers between devices  37.4 us
    all_gather x1, blocking collectives, local(): home_states = lax.all_gather(compact, 'req', axis=0, tiled=True)  25.4 us
    all_gather x1, waiting for transfers between devices, local(): lax.all_gather(normed, 'req', axis=0, tiled=True)  23.6 us
    all_gather x1, blocking collectives, local(): lax.all_gather(merged[2], 'tp', axis=0, tiled=True)  12.5 us
    dot_general x1, matrix products, local(): lax.dot_general(lax.all_gather(normed, 'req', axis=0, tiled=True), head_w...  12.1 us
    all_gather x1, blocking collectives, local(): lax.all_gather(merged[0], 'tp', axis=0, tiled=True)  12 us
    all_gather x1, blocking collectives, local(): lax.all_gather(merged[1], 'tp', axis=0, tiled=True)  12 us
  transfers between devices with their start and end apart: 2, of which 2 were waited for; matrix products, arithmetic and copies ran while one was open for 1% of the time, Pallas kernels for 0%

commit v1 on v0

--- a/solution.py
+++ b/solution.py
@@ -8,6 +8,27 @@
 EPS = 1e-05
 HIGH = lax.Precision.HIGHEST
 block_limit = 512
+
+
+def collect(x, axis, dim):
+    length, index, rows = (lax.axis_size(axis), lax.axis_index(axis), x.shape[dim])
+    right = [(i, (i + 1) % length) for i in range(length)]
+    behind = [(i, (i - 1) % length) for i in range(length)]
+    filled = jnp.zeros((*x.shape[:dim], length * rows, *x.shape[dim + 1 :]), x.dtype)
+    filled = lax.dynamic_update_slice_in_dim(filled, x, index * rows, axis=dim)
+    from_left = from_right = x
+    half = length // 2
+    for hop in range(1, half + 1):
+        from_left = lax.ppermute(from_left, axis, right)
+        filled = lax.dynamic_update_slice_in_dim(
+            filled, from_left, (index - hop) % length * rows, axis=dim
+        )
+        if hop < length - half:
+            from_right = lax.ppermute(from_right, axis, behind)
+            filled = lax.dynamic_update_slice_in_dim(
+                filled, from_right, (index + hop) % length * rows, axis=dim
+            )
+    return filled
 
 
 def combined_all(value, axis, join):
@@ -169,7 +190,7 @@
     local_stats = tuple((after_part for after_part in found_stats))
     merged = combined_all((local_stats[0], local_stats[1], local_stats[2]), "req", combine_stats)
     all_stats = (
-        lax.all_gather(merged[0], "tp", axis=0, tiled=True),
+        collect(merged[0], "tp", 0),
         lax.all_gather(merged[1], "tp", axis=0, tiled=True),
         lax.all_gather(merged[2], "tp", axis=0, tiled=True),
     )

time: 276 us -> 269 us (0.975)
  blocking collectives: 150 us -> 137 us
  starting transfers between devices: 0.08 us -> 3.91 us
    all_gather x1 -> x0, blocking collectives: 12 us -> none  [local(): lax.all_gather(merged[0], 'tp', axis=0, tiled=True)]
    ppermute x0 -> x3, starting transfers between devices: none -> 3.83 us  [the longest x2 2.15 us: collect(): from_left = lax.ppermute(from_left, axis, right)]
  transfers between devices with their start and end apart: 2 -> 5, of which waited for: 2 -> 2; matrix products, arithmetic and copies ran while one was open for 1% -> 1% of each run, Pallas kernels for 0% -> 0%
where the time goes in v1:
time: 269 us; the launch traced here: 268 us
  blocking collectives  137 us (51%)
  waiting for transfers between devices  61 us (23%)
  matrix products  22.3 us (8%)
  local copies, waits for them, and re-layouts  21.4 us (8%)
  between operations  15.1 us (6%)
  other arithmetic  5.42 us (2%)
  starting transfers between devices  3.91 us (1%)
    all_gather x3, blocking collectives, combined_all(): pieces = jax.tree.map(lambda part: lax.all_gather(part, axis), value)  70.6 us
    unnamed x3, waiting for transfers between devices  37.4 us
    all_gather x1, blocking collectives, local(): home_states = lax.all_gather(compact, 'req', axis=0, tiled=True)  25.4 us
    all_gather x1, waiting for transfers between devices, local(): lax.all_gather(normed, 'req', axis=0, tiled=True)  23.5 us
    dot_general x1, matrix products, local(): lax.dot_general(lax.all_gather(normed, 'req', axis=0, tiled=True), head_w...  12.1 us
    all_gather x1, blocking collectives, local(): lax.all_gather(merged[2], 'tp', axis=0, tiled=True)  12 us
    all_gather x1, blocking collectives, local(): lax.all_gather(merged[1], 'tp', axis=0, tiled=True)  12 us
    all_to_all x1, blocking collectives, local(): lax.all_to_all(normed_slice, 'tp', split_axis=0, concat_axis=1, tiled=True)  9.35 us
  transfers between devices with their start and end apart: 5, of which 2 were waited for; matrix products, arithmetic and copies ran while one was open for 1% of the time, Pallas kernels for 0%

profile of v1, /device:TPU:0, one launch (start us, length us, event | category | flops | bytes accessed | tf_op | source)
XLA Modules:
  0.0 267.8 jit_solution(12670442148931357687)
XLA Ops:
  7.2 1.4 reduce_max.37
  9.3 1.0 fusion.21
  10.3 0.2 fusion.38
  10.5 0.9 fusion.22
  11.4 0.2 fusion.37
  11.6 0.2 fusion.39
  11.8 0.1 copy.47
  11.9 1.2 reshape.97
  13.1 0.7 copy.48
  13.9 1.2 reshape.98
  15.1 1.2 reshape.99
  16.3 0.2 fusion.35
  16.5 0.1 fusion.18
  16.6 0.3 fusion.13
  16.9 12.5 %while.28 = (s32[]{:T(128)}, f32[2,4,64]{2,1,0:T(4,128)S(1)}, f32[2,4,64]{2,1,0:T(4,128)S(1)}, f32[2,4,64,224]{3,2,1,0:T(8,128)S(1)}, s32[]{:T(128)}, /*index=5*...) while((s32[]{:T(128)}, f32[2,4,64]{2,1,0:T(4,128)S(1)}, ...), condition=%wide.region_6.7_spmd, body=%wide.region_3.6_spmd.sunk | while | flops 236947968 | bytes 23599292 | solution.py:150
  16.9 0.1 broadcast_compare_fusion.2
  17.0 4.1 %constant_dynamic-slice_fusion.9 = (bf16[2,512,896]{2,1,0:T(8,128)(2,1)}, bf16[2,512,896]{2,1,0:T(8,128)(2,1)}) fusion(bf16[2,1024,896]{2,1,0:T(8,128)(2,1)} %get-tuple-element.346, s32[]{:T(128)S(6)} %select_n.75, bf16[2,1024,896]{2,1,0:T(8,128)(2,1)} %get-tuple-element.344), kind=kLoop, calls=%fused_computation.13.clone.1 | loop fusion | bytes 7340036 | tf_op jit(solution)/shard_map/while/body/dynamic_slice | solution.py:124
  21.1 2.7 %copy.80 = bf16[2,512,896]{1,2,0:T(8,128)(2,1)S(1)} copy(bf16[2,512,896]{2,1,0:T(8,128)(2,1)} %get-tuple-element.295) | data formatting | bytes 3670016 | tf_op jit(solution)/shard_map/while/body/dynamic_slice | solution.py:121
  23.9 1.5 fusion.66
  25.4 0.3 fusion.67
  25.8 2.8 %copy.81 = bf16[2,512,896]{1,2,0:T(8,128)(2,1)S(1)} copy(bf16[2,512,896]{2,1,0:T(8,128)(2,1)} %get-tuple-element.300) | data formatting | bytes 3670016 | tf_op jit(solution)/shard_map/while/body/dynamic_slice | solution.py:124
  28.5 0.7 fusion.68
  29.2 0.2 multiply_add_fusion.7
  29.4 0.1 fusion.16
  29.6 0.2 copy.55
  29.8 0.2 reshape.100
  30.0 4.0 %convolution_convert_fusion = bf16[128,3584]{1,0:T(8,128)(2,1)S(1)} fusion(bf16[128,896]{1,0:T(8,128)(2,1)S(1)} %reshape.100, bf16[896,3584]{1,0:T(8,128)(2,1)} %param.27), kind=kOutput, calls=%fused_computation.19 | convolution fusion | flops 822542336 | bytes 7569408 | tf_op jit(solution)/shard_map/dot_general | solution.py:159
  34.0 1.3 copy.61
  35.3 0.0 all-gather.5.cloned.1.call-start
  35.4 0.8 dynamic_slice.26
  36.1 37.4 %reduce-scatter.4.cloned.1.call-done = bf16[896,128]{1,0:T(8,128)(2,1)} async-done(((bf16[3584,128]{1,0:T(8,128)(2,1)}), bf16[896,128]{1,0:T(8,128)(2,1)}) %reduce-scatter.4.cloned.1.call-update) | async-done | bytes 229392
  73.5 1.1 copy.62
  74.6 1.1 fusion.10
  75.7 8.0 %psum.7 = f32[128]{0:T(128)S(1)} all-reduce(f32[128]{0:T(128)S(1)} %get-tuple-element.177), channel_id=1, replica_groups=mesh['req'=32,'tp'=4] {'tp'}, use_global_device_ids=true, to_apply=%region_9.10 | all-reduce | flops 128 | bytes 1024 | tf_op jit(solution)/shard_map/psum | solution.py:167
  83.7 0.1 fusion.12
  83.9 9.3 %all_to_all.19 = bf16[4,32,896]{2,1,0:T(8,128)(2,1)S(1)} all-to-all(bf16[4,32,896]{2,1,0:T(8,128)(2,1)S(1)} %bitcast.79), channel_id=1, replica_groups=mesh['req'=32,'tp'=4] {'tp'}, dimensions={0} | all-to-all | bytes 458752 | tf_op jit(solution)/shard_map/all_to_all | solution.py:177
  93.2 0.7 copy.65
  94.0 0.1 reshape.101
  94.1 0.1 constant_dynamic-slice_fusion.5
  94.2 0.1 eq.58
  94.2 0.1 fusion.8
  94.4 25.4 %all_gather.39 = bf16[64,8,896]{2,1,0:T(8,128)(2,1)S(1)} all-gather(bf16[2,8,896]{2,1,0:T(8,128)(2,1)S(1)} %fusion.8), channel_id=1, replica_groups=mesh['req'=32,'tp'=4] {'req'}, dimensions={0}, use_global_device_ids=true | all-gather | bytes 946176 | tf_op jit(solution)/shard_map/all_gather | solution.py:207
  119.8 0.3 convolution_convert_fusion.1
  120.1 0.6 copy.59
  120.7 23.5 %all-gather.5.cloned.1.call-done = bf16[1024,3584]{1,0:T(8,128)(2,1)} async-done(((bf16[32,3584]{1,0:T(8,128)(2,1)}), bf16[1024,3584]{1,0:T(8,128)(2,1)}) %all-gather.5.cloned.1.call-update) | async-done | bytes 7340048 | tf_op jit(solution)/shard_map/all_gather | solution.py:184
  144.2 12.1 %fusion.36 = (f32[1024]{0:T(1024)S(1)}, f32[1024,1000]{0,1:T(8,128)S(1)}) fusion(bf16[1024,3584]{1,0:T(8,128)(2,1)} %all-gather.5.cloned.1.call-done, bf16[1000,3584]{1,0:T(8,128)(2,1)} %param.29), kind=kOutput, calls=%fused_computation.70 | convolution fusion | flops 7341054976 | bytes 18608128 | tf_op jit(solution)/shard_map/dot_general | solution.py:183
  156.3 1.4 select_reduce_fusion
  157.7 24.1 %all-gather.2 = f32[32768]{0:T(1024)S(1)} all-gather(f32[1024]{0:T(1024)S(1)} %get-tuple-element.139), channel_id=4, replica_groups=mesh['req'=32,'tp'=4] {'req'}, dimensions={0}, use_global_device_ids=true | all-gather | bytes 135168 | tf_op jit(solution)/shard_map/all_gather | solution.py:35
  181.8 22.7 %all-gather = f32[32768]{0:T(1024)S(1)} all-gather(f32[1024]{0:T(1024)S(1)} %get-tuple-element.187), channel_id=2, replica_groups=mesh['req'=32,'tp'=4] {'req'}, dimensions={0}, use_global_device_ids=true | all-gather | bytes 135168 | tf_op jit(solution)/shard_map/all_gather | solution.py:35
  204.5 23.8 %all-gather.1 = f32[32768]{0:T(1024)S(1)} all-gather(f32[1024]{0:T(1024)S(1)} %get-tuple-element.140), channel_id=3, replica_groups=mesh['req'=32,'tp'=4] {'req'}, dimensions={0}, use_global_device_ids=true | all-gather | bytes 135168 | tf_op jit(solution)/shard_map/all_gather | solution.py:35
  228.4 2.8 %while.29 = (s32[]{:T(128)}, f32[1024]{0:T(1024)S(1)}, f32[1024]{0:T(1024)S(1)}, f32[1024]{0:T(1024)S(1)}, f32[31,1024]{1,0:T(8,128)S(1)}, /*index=5*/f32[31,1024]{1,0:T(8,128)S(1)}, f32[31,1024]{1,0:T(8,128)S(1)}, s32[]{:T(128)}) while((s32[]{:T(128)}, f32[1024]{0:T(1024)S(1)}, f32[1024]{0:T(1024)S(1)}, f32[1024]{0:T(1024)S(1)}, ...), condition=%wide.region_14.15_spmd, body=%wide.region_13.14_spmd.sunk | while | flops 7170 | bytes 61541 | solution.py:38
  231.2 1.6 collective-permute-start
  232.9 1.7 collective-permute-start.1
  234.6 0.2 dynamic_update_slice.12
  234.7 12.0 %all_gather.37 = f32[4096]{0:T(1024)S(1)} all-gather(f32[1024]{0:T(1024)S(1)} %get-tuple-element.92), channel_id=1, replica_groups=mesh['req'=32,'tp'=4] {'tp'}, dimensions={0}, use_global_device_ids=true | all-gather | bytes 20480 | tf_op jit(solution)/shard_map/all_gather | solution.py:195
  246.7 0.5 collective-permute-start.2
  247.3 12.0 %all_gather.38 = f32[4096]{0:T(1024)S(1)} all-gather(f32[1024]{0:T(1024)S(1)} %get-tuple-element.94), channel_id=1, replica_groups=mesh['req'=32,'tp'=4] {'tp'}, dimensions={0}, use_global_device_ids=true | all-gather | bytes 20480 | tf_op jit(solution)/shard_map/all_gather | solution.py:194
  259.3 0.2 dynamic_update_slice.13
  259.4 0.3 dynamic_update_slice.14
  259.7 0.3 dynamic_update_slice.15
  260.0 0.1 sub.76
  260.1 0.1 copy.57
  260.1 0.1 sub.78
  260.2 0.8 fusion.27
  (159 shorter events, 1.8 us)
Async XLA Ops:
  7.2 9.7 %copy-start.1 = (s32[2]{0:T(128)S(1)}, s32[2]{0:T(128)}, u32[]{:S(2)}) copy-start(s32[2]{0:T(128)} %param.24) | copy-start | bytes 28
  7.2 66.4 %reduce-scatter.4.cloned.1.call-start = ((), (), s32[]{:S(2)}) async-start(), calls=%async_computation.3 | async-start | bytes 1146880
  34.0 60.0 %copy-start = (s32[64,64]{1,0:T(8,128)S(1)}, s32[64,64]{1,0:T(8,128)}, u32[]{:S(2)}) copy-start(s32[64,64]{1,0:T(8,128)} %param.30) | copy-start | bytes 49156
  34.0 60.3 %copy-start.2 = (s32[2,8,64]{2,1,0:T(8,128)S(1)}, s32[2,8,64]{2,1,0:T(8,128)}, u32[]{:S(2)}) copy-start(s32[2,8,64]{2,1,0:T(8,128)} %param.26) | copy-start | bytes 12292
  34.0 85.8 %copy-start.3 = (s32[64]{0:T(128)S(1)}, s32[64]{0:T(128)}, u32[]{:S(2)}) copy-start(s32[64]{0:T(128)} %param.31) | copy-start | bytes 772
  35.3 108.9 %all-gather.5.cloned.1.call-start = ((), (), s32[]{:S(2)}) async-start(), calls=%async_computation.2 | async-start | bytes 7569408 | tf_op jit(solution)/shard_map/all_gather | solution.py:184
  231.2 15.5 %collective-permute-start = (f32[1024]{0:T(1024)S(1)}, f32[1024]{0:T(1024)S(1)}, u32[]{:S(2)}, u32[]{:S(2)}) collective-permute-start(f32[1024]{0:T(1024)S(1)} %get-tuple-element.93), channel_id=1, source_target_pairs={{0,1},{1,2},{2,3},{3,0},{4,5},{5,6},{6,7},{7,4},{8,9},{9,10},{10,1... | collective-permute-start | bytes 12296 | tf_op jit(solution)/shard_map/ppermute | solution.py:22
  232.9 26.6 %collective-permute-start.1 = (f32[1024]{0:T(1024)S(1)}, f32[1024]{0:T(1024)S(1)}, u32[]{:S(2)}, u32[]{:S(2)}) collective-permute-start(f32[1024]{0:T(1024)S(1)} %get-tuple-element.93), channel_id=1, source_target_pairs={{0,3},{1,0},{2,1},{3,2},{4,7},{5,4},{6,5},{7,6},{8,11},{9,8},{10,9... | collective-permute-start | bytes 12296 | tf_op jit(solution)/shard_map/ppermute | solution.py:27
  246.7 13.0 %collective-permute-start.2 = (f32[1024]{0:T(1024)S(1)}, f32[1024]{0:T(1024)S(1)}, u32[]{:S(2)}, u32[]{:S(2)}) collective-permute-start(f32[1024]{0:T(1024)S(1)} %collective-permute-done), channel_id=1, source_target_pairs={{0,1},{1,2},{2,3},{3,0},{4,5},{5,6},{6,7},{7,4},{8,9},{9,10},{10,1... | collective-permute-start | bytes 12296 | tf_op jit(solution)/shard_map/ppermute | solution.py:22
Sparse Core Ops, SparseCore 0:
  35.4 38.0 reduce-scatter.3
  94.1 50.1 all-gather.4
